TPU v7x, 32 devices: a whole 2x2x4 slice. The times are simulated.
32 devices in a mesh: gx: 4 (over y, x), gy: 2 (over core), gz: 4 (over z).
Axes of the slice: x: 2, y: 2, z: 4, core: 2. Of those that a mesh axis runs over, the one named last changes fastest.
Arguments:
- features: bfloat16 [8, 32, 65536], P('gz', 'gy', 'gx'), may hold values from -6 to 6
- depth_weight: bfloat16 [27, 64], replicated, may hold values from -1.25 to 1.25
- expand_weight: bfloat16 [64, 256], replicated, may hold values from -0.75 to 0.75
- project_weight: bfloat16 [256, 64], replicated, may hold values from -0.375 to 0.375
- spec_real: bfloat16 [32, 64, 64], replicated, may hold values from -2 to 2
- spec_imag: bfloat16 [32, 64, 64], replicated, may hold values from -2 to 2
- cotangent: bfloat16 [8, 32, 65536], P('gz', 'gy', 'gx'), may hold values from -6 to 6
Outputs:
- output: bfloat16 [8, 32, 65536], P('gz', 'gy', 'gx')
- grad_features: bfloat16 [8, 32, 65536], P('gz', 'gy', 'gx')
- grad_spec: float32 [2, 32, 64, 64], P(None, 'gx')
All inputs are finite; a program needn't handle non-finite values.
Results may differ from a plain program's by a relative error of at most 0.018.
Values may be sent and summed in bfloat16 or wider, within the bound.
No kernel may reach another device: no remote copies, remote signals or barrier semaphores. Data moves between devices by JAX's collectives and lax.ppermute only.
A program may use at most 64 MiB of HBM per device.

v0:
```python
import math
import jax
import jax.numpy as jnp
from jax import lax
from jax.sharding import PartitionSpec as P


def padded_2(value, sides, width, wrap):
    for axis, dim in sides:
        size, length = (lax.axis_size(axis), value.shape[dim])
        up = [(i, (i + 1) % size) for i in range(size if wrap else size - 1)]
        down = [(j, i) for i, j in up]
        last = lax.slice_in_dim(value, length - width, length, axis=dim)
        leading = lax.slice_in_dim(value, 0, width, axis=dim)
        before = lax.ppermute(last, axis, up)
        after = lax.ppermute(leading, axis, down)
        value = jnp.concatenate([before, value, after], axis=dim)
    return value


def gelu_parts(values):
    normal_cdf = 0.5 * (1.0 + jax.scipy.special.erf(values * (1.0 / math.sqrt(2.0))))
    density = jnp.exp(-0.5 * values * values) * (1.0 / math.sqrt(2.0 * math.pi))
    return (values * normal_cdf, normal_cdf + values * density)


def dft_tables(offset, cells, x_length, mode_count):
    position = offset + jnp.arange(cells, dtype=jnp.int32)
    frequency = jnp.arange(mode_count, dtype=jnp.int32)
    phase_int = position[:, None] * frequency[None, :] % x_length
    angles = phase_int.astype(jnp.float32) * (2.0 * math.pi / x_length)
    return (jnp.cos(angles).astype(jnp.bfloat16), (-jnp.sin(angles)).astype(jnp.bfloat16))


def scaled_table(table, mode_count, x_length):
    frequency = jnp.arange(mode_count, dtype=jnp.int32)
    mode_scale = jnp.where(frequency == 0, 1.0, 2.0).astype(jnp.float32) / x_length
    return (table.astype(jnp.float32) * mode_scale[None, :]).astype(jnp.bfloat16)


def block_weights(spec_real, spec_imag):
    upper_row = jnp.concatenate([spec_real, spec_imag], axis=2)
    lower_row = jnp.concatenate([-spec_imag, spec_real], axis=2)
    return jnp.concatenate([upper_row, lower_row], axis=1)


def spatial_rims(field_block, channels):
    x_wide = padded_2(field_block, (("gx", 2),), channels, True)
    return padded_2(x_wide, (("gy", 1), ("gz", 0)), 1, False)


def depthwise(padded, taps, flipped, x_cells, channels):
    planes = padded.shape[0] - 2
    y_cells = padded.shape[1] - 2
    running = jnp.zeros((planes, y_cells, x_cells * channels), jnp.float32)
    direction = -1 if flipped else 1
    for step_z in (-1, 0, 1):
        for step_y in (-1, 0, 1):
            for step_x in (-1, 0, 1):
                tap_gain = taps[(step_z + 1) * 9 + (step_y + 1) * 3 + (step_x + 1)].astype(
                    jnp.float32
                )
                z_offset = 1 + direction * step_z
                y_offset = 1 + direction * step_y
                x_offset = 1 + direction * step_x
                cut = padded[
                    z_offset : z_offset + planes,
                    y_offset : y_offset + y_cells,
                    x_offset * channels : (x_offset + x_cells) * channels,
                ]
                running = running + cut.astype(jnp.float32) * jnp.tile(tap_gain, x_cells)
    return running


def share_terms(field3, cos_table, sin_table):
    real_part = jnp.einsum("rxc,xk->krc", field3, cos_table, preferred_element_type=jnp.float32)
    imag_part = jnp.einsum("rxc,xk->krc", field3, sin_table, preferred_element_type=jnp.float32)
    return lax.psum_scatter(
        jnp.concatenate([real_part, imag_part], axis=2), "gx", scatter_dimension=0, tiled=True
    )


def share_inverse(modes_share, cos_table, sin_table, channels):
    segment = lax.all_gather(modes_share, "gx", axis=0, tiled=True)
    running = jnp.einsum(
        "krc,xk->rxc", segment[:, :, :channels], cos_table, preferred_element_type=jnp.float32
    )
    return running + jnp.einsum(
        "krc,xk->rxc", segment[:, :, channels:], sin_table, preferred_element_type=jnp.float32
    )


def split_gradients(dblock, channels):
    grad_real = dblock[:, :channels, :channels] + dblock[:, channels:, channels:]
    grad_imag = dblock[:, :channels, channels:] - dblock[:, channels:, :channels]
    return jnp.stack([grad_real, grad_imag])


def sum_gradients(local_grads):
    return lax.psum(local_grads.astype(jnp.bfloat16), ("gy", "gz")).astype(jnp.float32)


def per_device(
    features, depth_weight, expand_weight, project_weight, spec_real, spec_imag, cotangent
):
    planes, y_cells, merged = features.shape
    channels = depth_weight.shape[1]
    x_cells = merged // channels
    row_count = planes * y_cells
    mode_count = spec_real.shape[0]
    group_size = lax.axis_size("gx")
    x_length = x_cells * group_size
    x_start = lax.axis_index("gx") * x_cells
    cos_part, sin_part = dft_tables(x_start, x_cells, x_length, mode_count)
    cos_scaled = scaled_table(cos_part, mode_count, x_length)
    sin_scaled = scaled_table(sin_part, mode_count, x_length)
    blocks = block_weights(spec_real, spec_imag)
    padded = spatial_rims(features, channels)
    activation = depthwise(padded, depth_weight, False, x_cells, channels).astype(jnp.bfloat16)
    activation = activation.reshape(row_count * x_cells, channels)
    hidden_pre = jnp.dot(activation, expand_weight, preferred_element_type=jnp.float32)
    hidden, hidden_slope = gelu_parts(hidden_pre)
    local_branch = jnp.dot(
        hidden.astype(jnp.bfloat16), project_weight, preferred_element_type=jnp.float32
    )
    local_branch = local_branch.reshape(row_count, x_cells, channels)
    field3 = features.reshape(row_count, x_cells, channels)
    share_size = mode_count // group_size
    owned_blocks = lax.dynamic_slice_in_dim(
        blocks, lax.axis_index("gx") * share_size, share_size, 0
    )
    coeffs = share_terms(field3, cos_part, sin_part).astype(jnp.bfloat16)
    mixed_modes = jnp.einsum(
        "krc,kco->kro", coeffs, owned_blocks, preferred_element_type=jnp.float32
    ).astype(jnp.bfloat16)
    spectral = share_inverse(mixed_modes, cos_scaled, sin_scaled, channels)
    result, slopes = gelu_parts(local_branch + spectral)
    output = result.astype(jnp.bfloat16).reshape(planes, y_cells, merged)
    grad_pre = (
        cotangent.reshape(row_count, x_cells, channels).astype(jnp.float32) * slopes
    ).astype(jnp.bfloat16)
    hidden_grad = jnp.dot(
        grad_pre.reshape(row_count * x_cells, channels),
        project_weight.T,
        preferred_element_type=jnp.float32,
    )
    grad_hidden = (hidden_grad * hidden_slope).astype(jnp.bfloat16)
    grad_act = jnp.dot(grad_hidden, expand_weight.T, preferred_element_type=jnp.float32).astype(
        jnp.bfloat16
    )
    grad_act = grad_act.reshape(planes, y_cells, merged)
    dcoef = share_terms(grad_pre, cos_scaled, sin_scaled).astype(jnp.bfloat16)
    dmode = jnp.einsum(
        "kro,kco->krc", dcoef, owned_blocks, preferred_element_type=jnp.float32
    ).astype(jnp.bfloat16)
    spectral_grad = share_inverse(dmode, cos_part, sin_part, channels)
    dblock = jnp.einsum("krc,kro->kco", coeffs, dcoef, preferred_element_type=jnp.float32)
    grad_spec = sum_gradients(split_gradients(dblock, channels))
    padded_grad = spatial_rims(grad_act, channels)
    grad_local = depthwise(padded_grad, depth_weight, True, x_cells, channels)
    grad_features = (grad_local + spectral_grad.reshape(planes, y_cells, merged)).astype(
        jnp.bfloat16
    )
    return (output, grad_features, grad_spec)


def solution(mesh):
    placed = (P("gz", "gy", "gx"), P(), P(), P(), P(), P(), P("gz", "gy", "gx"))
    return jax.shard_map(
        per_device,
        mesh=mesh,
        in_specs=placed,
        out_specs=(P("gz", "gy", "gx"), P("gz", "gy", "gx"), P(None, "gx", None, None)),
        check_vma=False,
    )
```

profile of v0, /device:TPU:0, one launch (start us, length us, event | category | flops | bytes accessed | tf_op | source)
XLA Modules:
  0.0 243.0 jit_solution(9802269547435364776)
XLA Ops:
  8.0 3.9 %collective-permute-start.1 = (bf16[2,16,64]{2,1,0:T(8,128)(2,1)S(1)}, bf16[2,16,64]{2,1,0:T(8,128)(2,1)S(1)}, u32[]{:S(2)}, u32[]{:S(2)}) collective-permute-start(bf16[2,16,64]{2,1,0:T(8,128)(2,1)S(1)} %get-tuple-element.19), channel_id=1, source_target_pairs={{8,0},{16,8},{24,16},{0,24},{9,1},{17,9},{25,17},{1,25},{10,2},{18... | collective-permute-start | bytes 12296 | tf_op jit(solution)/shard_map/ppermute | solution.py:16
  11.9 3.0 %reshape.69 = bf16[32,256,64]{2,1,0:T(8,128)(2,1)S(1)} reshape(bf16[2,16,16384]{2,1,0:T(8,128)(2,1)} %param.7) | data formatting | bytes 2097152 | tf_op jit(solution)/shard_map/reshape | solution.py:127
  15.0 1.4 fusion.47
  16.3 1.3 fusion.50
  17.7 2.8 %concatenate.105 = bf16[2,16,16512]{2,1,0:T(8,128)(2,1)S(1)} concatenate(bf16[2,16,64]{2,1,0:T(8,128)(2,1)S(1)} %collective-permute-done, bf16[2,16,16384]{2,1,0:T(8,128)(2,1)} %param.7, bf16[2,16,64]{2,1,0:T(8,128)(2,1)S(1)} %collective-permute-done.1), dimensions={2} | concatenate | bytes 2113536 | tf_op jit(solution)/shard_map/concatenate | solution.py:17
  20.7 1.5 collective-permute-start.2
  22.2 1.3 collective-permute-start.3
  26.1 1.2 fusion.94
  27.3 4.4 %collective-permute-start.4 = (bf16[1,18,16512]{2,1,0:T(8,128)(2,1)}, bf16[1,18,16512]{2,1,0:T(8,128)(2,1)}, u32[]{:S(2)}, u32[]{:S(2)}) collective-permute-start(bf16[1,18,16512]{2,1,0:T(8,128)(2,1)} %get-tuple-element.7), channel_id=1, source_target_pairs={{0,1},{1,2},{2,3},{4,5},{5,6},{6,7},{8,9},{9,10},{10,11},{12,13},{... | collective-permute-start | bytes 1783304 | tf_op jit(solution)/shard_map/ppermute | solution.py:15
  31.7 1.5 collective-permute-start.5
  52.3 3.3 %reshape.101 = f32[32,256,64]{2,1,0:T(8,128)} reshape(bf16[2,16,16384]{2,1,0:T(8,128)(2,1)S(1)} %copy-done.13) | data formatting | bytes 3145728 | tf_op jit(solution)/shard_map/convert_element_type | solution.py:140
  55.6 3.9 %copy.44 = f32[32,256,64]{1,2,0:T(8,128)} copy(f32[32,256,64]{2,1,0:T(8,128)} %reshape.101) | data formatting | bytes 4194304 | tf_op jit(solution)/shard_map/convert_element_type | solution.py:140
  59.9 3.0 %maximum_maximum_fusion = (bf16[3,18,16512]{2,1,0:T(8,128)(2,1)S(1)}, bf16[3,18,16512]{2,1,0:T(8,128)(2,1)S(1)}) fusion(bf16[2,1,16512]{2,1,0:T(2,128)(2,1)S(1)} %collective-permute-done.3, bf16[2,16,16512]{2,1,0:T(8,128)(2,1)S(1)} %concatenate.105, bf16[2,1,16512]{2,1,0:T(2,128)(2,1)S(1)} %collective-permute-done.2, ...), kind=kLoop, calls=%fused_computation.12 | loop fusion | flops 14266368 | bytes 5944320 | tf_op jit(solution)/shard_map/concatenate | solution.py:17
  63.2 14.8 %add_convert_fusion.1 = bf16[2,16,16384]{2,1,0:T(8,128)(2,1)} fusion(bf16[2,16,16384]{2,1,0:T(8,128)(2,1)S(1)} %copy-done.3, bf16[2,16,16512]{2,1,0:T(8,128)(2,1)S(1)} %concatenate.105, bf16[2,1,16512]{2,1,0:T(2,128)(2,1)S(1)} %collective-permute-done.3, bf16[2,1,16512]{2,1,0:T(2,128)(2,1)S(1)} %collective-permute-done.2, ...), kind=kLoop, calls=%fused_computation.35 | loop fusion | flops 55050240 | bytes 23938048 | tf_op jit(solution)/shard_map/convert_element_type | solution.py:119
  78.0 3.0 %reshape.67 = bf16[8192,64]{1,0:T(8,128)(2,1)S(1)} reshape(bf16[2,16,16384]{2,1,0:T(8,128)(2,1)} %add_convert_fusion.1) | data formatting | bytes 2097152 | tf_op jit(solution)/shard_map/reshape | solution.py:120
  81.0 1.2 fusion.101
  82.3 3.3 %copy-done.2 = f32[8192,256]{1,0:T(8,128)} copy-done((f32[8192,256]{1,0:T(8,128)}, f32[8192,256]{1,0:T(8,128)S(1)}, u32[]{:S(2)}) %copy-start.2) | copy-done | bytes 8388632
  85.6 3.4 %fusion.5 = f32[8192,64]{0,1:T(8,128)} fusion(bf16[256,64]{0,1:T(8,128)(2,1)S(1)} %copy-done.44, f32[8192,256]{1,0:T(8,128)S(1)} %fusion.101), kind=kOutput, calls=%fused_computation.10 | convolution fusion | flops 278921216 | bytes 10518528 | tf_op jit(solution)/shard_map/dot_general | solution.py:123
  90.9 9.6 %all_gather.6 = bf16[32,32,128]{2,1,0:T(8,128)(2,1)S(1)} all-gather(bf16[8,32,128]{2,1,0:T(8,128)(2,1)S(1)} %convolution_convert_fusion.2), channel_id=1, replica_groups=mesh['gx'=4,'gy'=2,'gz'=4] {'gx'}, dimensions={0}, use_global_device_ids=true | all-gather | bytes 327680 | tf_op jit(solution)/shard_map/all_gather | solution.py:84
  101.2 2.5 %fusion.11 = (bf16[32,256,64]{1,2,0:T(8,128)(2,1)S(1)}, bf16[32,256,64]{1,2,0:T(8,128)(2,1)}) fusion(f32[32,256,64]{1,2,0:T(8,128)S(1)} %copy-done.5, f32[256,32,64]{0,2,1:T(8,128)S(1)} %fusion.29, bf16[32,32,64]{2,1,0:T(8,128)(2,1)S(1)} %get-tuple-element.25, f32[32]{0:T(128)S(1)} %fusion.66, s32[256]{0:T(256)S(1)} %iota_add_fusion, ...), kind=kOutput, calls=%fused_computation.29 | convolution fusion | flops 41050112 | bytes 8520832 | tf_op jit(solution)/shard_map/krc,xk->rxc/dot_general | solution.py:88
  104.5 7.8 %convolution_convert_fusion = bf16[8192,64]{0,1:T(8,128)(2,1)S(1)} fusion(bf16[64,256]{1,0:T(8,128)(2,1)S(1)} %copy-done, bf16[8192,64]{0,1:T(8,128)(2,1)S(1)} %bitcast.128, bf16[256,64]{0,1:T(8,128)(2,1)S(1)} %copy-done.45, f32[8192,256]{1,0:T(8,128)} %copy-done.2), kind=kOutput, calls=%fused_computation.3 | convolution fusion | flops 558366720 | bytes 10551296 | tf_op jit(solution)/shard_map/dot_general | solution.py:148
  112.4 1.8 copy.46
  114.2 2.8 %reshape.72 = bf16[2,16,16384]{2,1,0:T(8,128)(2,1)S(1)} reshape(bf16[8192,64]{1,0:T(8,128)(2,1)} %copy.46) | data formatting | bytes 2097152 | tf_op jit(solution)/shard_map/reshape | solution.py:151
  117.1 1.5 collective-permute-start.7
  119.1 1.6 collective-permute-done.7
  120.8 2.4 collective-permute-done.6
  123.1 1.1 concatenate.117
  124.5 1.3 collective-permute-start.9
  125.8 3.0 %collective-permute-start.8 = (bf16[2,1,16512]{2,1,0:T(2,128)(2,1)S(1)}, bf16[2,1,16512]{2,1,0:T(2,128)(2,1)S(1)}, u32[]{:S(2)}, u32[]{:S(2)}) collective-permute-start(bf16[2,1,16512]{2,1,0:T(2,128)(2,1)S(1)} %get-tuple-element.14), channel_id=1, source_target_pairs={{0,4},{1,5},{2,6},{3,7},{8,12},{9,13},{10,14},{11,15},{16,20},{17,... | collective-permute-start | bytes 198152 | tf_op jit(solution)/shard_map/ppermute | solution.py:15
  130.4 1.3 fusion.93
  131.7 1.3 collective-permute-start.10
  133.0 6.1 %collective-permute-start.11 = (bf16[1,18,16512]{2,1,0:T(8,128)(2,1)}, bf16[1,18,16512]{2,1,0:T(8,128)(2,1)}, u32[]{:S(2)}, u32[]{:S(2)}) collective-permute-start(bf16[1,18,16512]{2,1,0:T(8,128)(2,1)} %get-tuple-element.6), channel_id=1, source_target_pairs={{0,1},{1,2},{2,3},{4,5},{5,6},{6,7},{8,9},{9,10},{10,11},{12,13},{... | collective-permute-start | bytes 1783304 | tf_op jit(solution)/shard_map/ppermute | solution.py:15
  141.5 2.0 copy.43
  143.6 2.5 %reshape.70 = bf16[2,16,16384]{2,1,0:T(8,128)(2,1)} reshape(bf16[32,256,64]{2,1,0:T(8,128)(2,1)S(1)} %copy.43) | data formatting | bytes 2097152 | tf_op jit(solution)/shard_map/reshape | solution.py:138
  146.1 8.7 %collective-permute-done.10 = bf16[1,18,16512]{2,1,0:T(8,128)(2,1)} collective-permute-done((bf16[1,18,16512]{2,1,0:T(8,128)(2,1)}, bf16[1,18,16512]{2,1,0:T(8,128)(2,1)}, u32[]{:S(2)}, u32[]{:S(2)}) %collective-permute-start.10) | collective-permute-done | bytes 594464 | tf_op jit(solution)/shard_map/ppermute | solution.py:16
  154.8 1.2 collective-permute-done.11
  156.0 3.9 %pad_maximum_fusion.1 = (bf16[3,18,16512]{2,1,0:T(8,128)(2,1)S(1)}, bf16[3,18,16512]{2,1,0:T(8,128)(2,1)}) fusion(bf16[1,18,16512]{2,1,0:T(8,128)(2,1)} %collective-permute-done.10, bf16[2,1,16512]{2,1,0:T(2,128)(2,1)} %copy-done.11, bf16[2,16,16512]{2,1,0:T(8,128)(2,1)S(1)} %concatenate.117, bf16[2,1,16512]{2,1,0:T(2,128)(2,1)} %copy-done.12, ...), kind=kLoop, calls=%fused_computation.14 | loop fusion | flops 14266368 | bytes 5944320 | tf_op jit(solution)/shard_map/concatenate | solution.py:17
  159.9 5.4 %reduce-scatter.5.cloned.1.call-done = f32[8,32,128]{2,0,1:T(8,128)} async-done(((f32[32,32,128]{2,0,1:T(8,128)}), f32[8,32,128]{2,0,1:T(8,128)}) %reduce-scatter.5.cloned.1.call-update) | async-done | bytes 131088 | tf_op jit(solution)/shard_map/reduce_scatter | solution.py:78
  166.2 1.2 convolution_convert_fusion.1
  167.4 1.1 fusion.33
  168.5 9.2 %all_gather.7 = bf16[32,32,128]{2,1,0:T(8,128)(2,1)S(1)} all-gather(bf16[8,32,128]{2,1,0:T(8,128)(2,1)S(1)} %convolution_convert_fusion.1), channel_id=1, replica_groups=mesh['gx'=4,'gy'=2,'gz'=4] {'gx'}, dimensions={0}, use_global_device_ids=true | all-gather | bytes 327680 | tf_op jit(solution)/shard_map/all_gather | solution.py:84
  179.6 1.6 fusion.26
  181.2 2.0 add_bitcast_fusion
  183.2 3.8 %copy.50 = f32[32,256,64]{2,1,0:T(8,128)} copy(f32[32,256,64]{1,2,0:T(8,128)} %add_bitcast_fusion) | data formatting | bytes 4194304 | tf_op jit(solution)/shard_map/add | solution.py:88
  187.0 4.0 %reshape.73 = f32[2,16,16384]{2,1,0:T(8,128)} reshape(f32[32,256,64]{2,1,0:T(8,128)} %copy.50) | data formatting | bytes 4194304 | tf_op jit(solution)/shard_map/reshape | solution.py:161
  191.0 21.6 %add_convert_fusion = bf16[2,16,16384]{2,1,0:T(8,128)(2,1)} fusion(f32[2,16,16384]{2,1,0:T(8,128)} %reshape.73, bf16[2,16,16384]{2,1,0:T(8,128)(2,1)} %copy-done.4, bf16[2,16,16512]{2,1,0:T(8,128)(2,1)S(1)} %concatenate.117, bf16[2,1,16512]{2,1,0:T(2,128)(2,1)} %copy-done.12, bf16[2,1,16512]{2,1,0:T(2,128)(2,1)} %copy-done.11, ...), kind=kLoop, calls=%fused_computation.31 | loop fusion | flops 55574528 | bytes 26035200 | tf_op jit(solution)/shard_map/convert_element_type | solution.py:161
  212.5 22.1 %all-reduce.2.cloned.1.call-done = bf16[2,8,64,64]{3,2,1,0:T(8,128)(2,1)} async-done(((bf16[2,8,64,64]{3,2,1,0:T(8,128)(2,1)}), bf16[2,8,64,64]{3,2,1,0:T(8,128)(2,1)}) %all-reduce.2.cloned.1.call-update) | async-done | bytes 131088 | tf_op jit(solution)/shard_map/psum | solution.py:100
  234.7 1.8 convert_element_type.381
  (187 shorter events, 33.7 us)
Async XLA Ops:
  7.2 73.9 %copy-start = (bf16[64,256]{1,0:T(8,128)(2,1)S(1)}, bf16[64,256]{1,0:T(8,128)(2,1)}, u32[]{:S(2)}) copy-start(bf16[64,256]{1,0:T(8,128)(2,1)} %param.9) | copy-start | bytes 98308
  7.2 81.8 %reduce-scatter.3.cloned.1.call-start = ((), (), s32[]{:S(2)}) async-start(), calls=%async_computation.2 | async-start | bytes 655360 | tf_op jit(solution)/shard_map/reduce_scatter | solution.py:78
  8.0 9.7 %collective-permute-start.1 = (bf16[2,16,64]{2,1,0:T(8,128)(2,1)S(1)}, bf16[2,16,64]{2,1,0:T(8,128)(2,1)S(1)}, u32[]{:S(2)}, u32[]{:S(2)}) collective-permute-start(bf16[2,16,64]{2,1,0:T(8,128)(2,1)S(1)} %get-tuple-element.19), channel_id=1, source_target_pairs={{8,0},{16,8},{24,16},{0,24},{9,1},{17,9},{25,17},{1,25},{10,2},{18... | collective-permute-start | bytes 12296 | tf_op jit(solution)/shard_map/ppermute | solution.py:16
  11.9 5.8 %collective-permute-start = (bf16[2,16,64]{2,1,0:T(8,128)(2,1)S(1)}, bf16[2,16,64]{2,1,0:T(8,128)(2,1)S(1)}, u32[]{:S(2)}, u32[]{:S(2)}) collective-permute-start(bf16[2,16,64]{2,1,0:T(8,128)(2,1)S(1)} %get-tuple-element.20), channel_id=1, source_target_pairs={{0,8},{8,16},{16,24},{24,0},{1,9},{9,17},{17,25},{25,1},{2,10},{10... | collective-permute-start | bytes 12296 | tf_op jit(solution)/shard_map/ppermute | solution.py:15
  17.7 5.8 %copy-start.8 = (f32[32,32,64]{2,0,1:T(8,128)S(1)}, f32[32,32,64]{2,0,1:T(8,128)}, u32[]{:S(2)}) copy-start(f32[32,32,64]{2,0,1:T(8,128)} %fusion.47) | copy-start | bytes 786436
  17.7 5.8 %copy-start.9 = (f32[32,32,64]{2,0,1:T(8,128)S(1)}, f32[32,32,64]{2,0,1:T(8,128)}, u32[]{:S(2)}) copy-start(f32[32,32,64]{2,0,1:T(8,128)} %fusion.50) | copy-start | bytes 786436
  20.7 3.9 %collective-permute-start.2 = (bf16[2,1,16512]{2,1,0:T(2,128)(2,1)S(1)}, bf16[2,1,16512]{2,1,0:T(2,128)(2,1)S(1)}, u32[]{:S(2)}, u32[]{:S(2)}) collective-permute-start(bf16[2,1,16512]{2,1,0:T(2,128)(2,1)S(1)} %get-tuple-element.15), channel_id=1, source_target_pairs={{0,4},{1,5},{2,6},{3,7},{8,12},{9,13},{10,14},{11,15},{16,20},{17,... | collective-permute-start | bytes 198152 | tf_op jit(solution)/shard_map/ppermute | solution.py:15
  22.2 3.2 %collective-permute-start.3 = (bf16[2,1,16512]{2,1,0:T(2,128)(2,1)S(1)}, bf16[2,1,16512]{2,1,0:T(2,128)(2,1)S(1)}, u32[]{:S(2)}, u32[]{:S(2)}) collective-permute-start(bf16[2,1,16512]{2,1,0:T(2,128)(2,1)S(1)} %get-tuple-element.16), channel_id=1, source_target_pairs={{4,0},{5,1},{6,2},{7,3},{12,8},{13,9},{14,10},{15,11},{20,16},{21,... | collective-permute-start | bytes 198152 | tf_op jit(solution)/shard_map/ppermute | solution.py:16
  24.5 140.8 %reduce-scatter.5.cloned.1.call-start = ((), (), s32[]{:S(2)}) async-start(), calls=%async_computation.3 | async-start | bytes 655360 | tf_op jit(solution)/shard_map/reduce_scatter | solution.py:78
  26.0 7.1 %copy-start.43 = (bf16[27,64]{1,0:T(8,128)(2,1)S(1)}, bf16[27,64]{1,0:T(8,128)(2,1)}, u32[]{:S(2)}) copy-start(bf16[27,64]{1,0:T(8,128)(2,1)} %param.8) | copy-start | bytes 10372
  27.3 32.6 %collective-permute-start.4 = (bf16[1,18,16512]{2,1,0:T(8,128)(2,1)}, bf16[1,18,16512]{2,1,0:T(8,128)(2,1)}, u32[]{:S(2)}, u32[]{:S(2)}) collective-permute-start(bf16[1,18,16512]{2,1,0:T(8,128)(2,1)} %get-tuple-element.7), channel_id=1, source_target_pairs={{0,1},{1,2},{2,3},{4,5},{5,6},{6,7},{8,9},{9,10},{10,11},{12,13},{... | collective-permute-start | bytes 1783304 | tf_op jit(solution)/shard_map/ppermute | solution.py:15
  31.7 28.2 %collective-permute-start.5 = (bf16[1,18,16512]{2,1,0:T(8,128)(2,1)}, bf16[1,18,16512]{2,1,0:T(8,128)(2,1)}, u32[]{:S(2)}, u32[]{:S(2)}) collective-permute-start(bf16[1,18,16512]{2,1,0:T(8,128)(2,1)} %get-tuple-element.8), channel_id=1, source_target_pairs={{1,0},{2,1},{3,2},{5,4},{6,5},{7,6},{9,8},{10,9},{11,10},{13,12},{... | collective-permute-start | bytes 1783304 | tf_op jit(solution)/shard_map/ppermute | solution.py:16
  42.7 9.5 %copy-start.10 = (bf16[32,64,64]{2,1,0:T(8,128)(2,1)S(1)}, bf16[32,64,64]{2,1,0:T(8,128)(2,1)}, u32[]{:S(2)}) copy-start(bf16[32,64,64]{2,1,0:T(8,128)(2,1)} %param.12) | copy-start | bytes 786436
  44.9 7.4 %copy-start.13 = (bf16[2,16,16384]{2,1,0:T(8,128)(2,1)S(1)}, bf16[2,16,16384]{2,1,0:T(8,128)(2,1)}, u32[]{:S(2)}) copy-start(bf16[2,16,16384]{2,1,0:T(8,128)(2,1)} %param.13) | copy-start | bytes 3145732
  55.6 3.9 %copy-start.42 = (bf16[32,64,64]{2,1,0:T(8,128)(2,1)S(1)}, bf16[32,64,64]{2,1,0:T(8,128)(2,1)}, u32[]{:S(2)}) copy-start(bf16[32,64,64]{2,1,0:T(8,128)(2,1)} %param.11) | copy-start | bytes 786436
  59.6 30.5 %copy-start.6 = (bf16[8,128,128]{2,1,0:T(8,128)(2,1)}, bf16[8,128,128]{2,1,0:T(8,128)(2,1)S(1)}, u32[]{:S(2)}) copy-start(bf16[8,128,128]{2,1,0:T(8,128)(2,1)S(1)} %fusion.21) | copy-start | bytes 786436
  59.6 3.3 %copy-start.3 = (bf16[2,16,16384]{2,1,0:T(8,128)(2,1)S(1)}, bf16[2,16,16384]{2,1,0:T(8,128)(2,1)}, u32[]{:S(2)}) copy-start(bf16[2,16,16384]{2,1,0:T(8,128)(2,1)} %param.7) | copy-start | bytes 3145732
  59.6 3.3 %copy-start.15 = (f32[16384]{0:T(1024)S(1)}, f32[16384]{0:T(1024)}, u32[]{:S(2)}) copy-start(f32[16384]{0:T(1024)} %mul.548) | copy-start | bytes 196612
  59.6 3.3 %copy-start.16 = (f32[16384]{0:T(1024)S(1)}, f32[16384]{0:T(1024)}, u32[]{:S(2)}) copy-start(f32[16384]{0:T(1024)} %mul.617) | copy-start | bytes 196612
  59.6 3.3 %copy-start.17 = (f32[16384]{0:T(1024)S(1)}, f32[16384]{0:T(1024)}, u32[]{:S(2)}) copy-start(f32[16384]{0:T(1024)} %mul.614) | copy-start | bytes 196612
  59.7 3.3 %copy-start.18 = (f32[16384]{0:T(1024)S(1)}, f32[16384]{0:T(1024)}, u32[]{:S(2)}) copy-start(f32[16384]{0:T(1024)} %mul.611) | copy-start | bytes 196612
  59.7 3.3 %copy-start.19 = (f32[16384]{0:T(1024)S(1)}, f32[16384]{0:T(1024)}, u32[]{:S(2)}) copy-start(f32[16384]{0:T(1024)} %mul.608) | copy-start | bytes 196612
  59.7 3.3 %copy-start.20 = (f32[16384]{0:T(1024)S(1)}, f32[16384]{0:T(1024)}, u32[]{:S(2)}) copy-start(f32[16384]{0:T(1024)} %mul.605) | copy-start | bytes 196612
  59.7 3.3 %copy-start.21 = (f32[16384]{0:T(1024)S(1)}, f32[16384]{0:T(1024)}, u32[]{:S(2)}) copy-start(f32[16384]{0:T(1024)} %mul.602) | copy-start | bytes 196612
  59.7 3.3 %copy-start.22 = (f32[16384]{0:T(1024)S(1)}, f32[16384]{0:T(1024)}, u32[]{:S(2)}) copy-start(f32[16384]{0:T(1024)} %mul.599) | copy-start | bytes 196612
  59.7 3.3 %copy-start.23 = (f32[16384]{0:T(1024)S(1)}, f32[16384]{0:T(1024)}, u32[]{:S(2)}) copy-start(f32[16384]{0:T(1024)} %mul.596) | copy-start | bytes 196612
  59.7 3.3 %copy-start.24 = (f32[16384]{0:T(1024)S(1)}, f32[16384]{0:T(1024)}, u32[]{:S(2)}) copy-start(f32[16384]{0:T(1024)} %mul.593) | copy-start | bytes 196612
  59.7 3.3 %copy-start.25 = (f32[16384]{0:T(1024)S(1)}, f32[16384]{0:T(1024)}, u32[]{:S(2)}) copy-start(f32[16384]{0:T(1024)} %mul.590) | copy-start | bytes 196612
  59.7 3.3 %copy-start.26 = (f32[16384]{0:T(1024)S(1)}, f32[16384]{0:T(1024)}, u32[]{:S(2)}) copy-start(f32[16384]{0:T(1024)} %mul.587) | copy-start | bytes 196612
  59.7 3.3 %copy-start.27 = (f32[16384]{0:T(1024)S(1)}, f32[16384]{0:T(1024)}, u32[]{:S(2)}) copy-start(f32[16384]{0:T(1024)} %mul.584) | copy-start | bytes 196612
  59.8 3.3 %copy-start.28 = (f32[16384]{0:T(1024)S(1)}, f32[16384]{0:T(1024)}, u32[]{:S(2)}) copy-start(f32[16384]{0:T(1024)} %mul.581) | copy-start | bytes 196612
  59.8 3.3 %copy-start.29 = (f32[16384]{0:T(1024)S(1)}, f32[16384]{0:T(1024)}, u32[]{:S(2)}) copy-start(f32[16384]{0:T(1024)} %mul.578) | copy-start | bytes 196612
  59.8 3.3 %copy-start.30 = (f32[16384]{0:T(1024)S(1)}, f32[16384]{0:T(1024)}, u32[]{:S(2)}) copy-start(f32[16384]{0:T(1024)} %mul.575) | copy-start | bytes 196612
  59.8 3.3 %copy-start.31 = (f32[16384]{0:T(1024)S(1)}, f32[16384]{0:T(1024)}, u32[]{:S(2)}) copy-start(f32[16384]{0:T(1024)} %mul.572) | copy-start | bytes 196612
  59.8 3.3 %copy-start.32 = (f32[16384]{0:T(1024)S(1)}, f32[16384]{0:T(1024)}, u32[]{:S(2)}) copy-start(f32[16384]{0:T(1024)} %mul.569) | copy-start | bytes 196612
  59.8 3.3 %copy-start.33 = (f32[16384]{0:T(1024)S(1)}, f32[16384]{0:T(1024)}, u32[]{:S(2)}) copy-start(f32[16384]{0:T(1024)} %mul.566) | copy-start | bytes 196612
  81.0 4.6 %copy-start.44 = (bf16[256,64]{0,1:T(8,128)(2,1)S(1)}, bf16[256,64]{0,1:T(8,128)(2,1)}, u32[]{:S(2)}) copy-start(bf16[256,64]{0,1:T(8,128)(2,1)} %param.10) | copy-start | bytes 98308
  89.0 12.2 %copy-start.7 = (f32[8192,64]{0,1:T(8,128)S(1)}, f32[8192,64]{0,1:T(8,128)}, u32[]{:S(2)}) copy-start(f32[8192,64]{0,1:T(8,128)} %fusion.5) | copy-start | bytes 6291460
  90.7 10.5 %copy-start.5 = (f32[32,256,64]{1,2,0:T(8,128)S(1)}, f32[32,256,64]{1,2,0:T(8,128)}, u32[]{:S(2)}) copy-start(f32[32,256,64]{1,2,0:T(8,128)} %copy.44) | copy-start | bytes 6291460
  117.0 13.4 %copy-start.4 = (bf16[2,16,16384]{2,1,0:T(8,128)(2,1)}, bf16[2,16,16384]{2,1,0:T(8,128)(2,1)S(1)}, u32[]{:S(2)}) copy-start(bf16[2,16,16384]{2,1,0:T(8,128)(2,1)S(1)} %reshape.72) | copy-start | bytes 3145732
  117.1 3.7 %collective-permute-start.7 = (bf16[2,16,64]{2,1,0:T(8,128)(2,1)S(1)}, bf16[2,16,64]{2,1,0:T(8,128)(2,1)S(1)}, u32[]{:S(2)}, u32[]{:S(2)}) collective-permute-start(bf16[2,16,64]{2,1,0:T(8,128)(2,1)S(1)} %get-tuple-element.17), channel_id=1, source_target_pairs={{8,0},{16,8},{24,16},{0,24},{9,1},{17,9},{25,17},{1,25},{10,2},{18... | collective-permute-start | bytes 12296 | tf_op jit(solution)/shard_map/ppermute | solution.py:16
  118.6 4.5 %collective-permute-start.6 = (bf16[2,16,64]{2,1,0:T(8,128)(2,1)S(1)}, bf16[2,16,64]{2,1,0:T(8,128)(2,1)S(1)}, u32[]{:S(2)}, u32[]{:S(2)}) collective-permute-start(bf16[2,16,64]{2,1,0:T(8,128)(2,1)S(1)} %get-tuple-element.18), channel_id=1, source_target_pairs={{0,8},{8,16},{16,24},{24,0},{1,9},{9,17},{17,25},{25,1},{2,10},{10... | collective-permute-start | bytes 12296 | tf_op jit(solution)/shard_map/ppermute | solution.py:15
  124.5 4.4 %collective-permute-start.9 = (bf16[2,1,16512]{2,1,0:T(2,128)(2,1)S(1)}, bf16[2,1,16512]{2,1,0:T(2,128)(2,1)S(1)}, u32[]{:S(2)}, u32[]{:S(2)}) collective-permute-start(bf16[2,1,16512]{2,1,0:T(2,128)(2,1)S(1)} %get-tuple-element.13), channel_id=1, source_target_pairs={{4,0},{5,1},{6,2},{7,3},{12,8},{13,9},{14,10},{15,11},{20,16},{21,... | collective-permute-start | bytes 198152 | tf_op jit(solution)/shard_map/ppermute | solution.py:16
  125.8 4.0 %collective-permute-start.8 = (bf16[2,1,16512]{2,1,0:T(2,128)(2,1)S(1)}, bf16[2,1,16512]{2,1,0:T(2,128)(2,1)S(1)}, u32[]{:S(2)}, u32[]{:S(2)}) collective-permute-start(bf16[2,1,16512]{2,1,0:T(2,128)(2,1)S(1)} %get-tuple-element.14), channel_id=1, source_target_pairs={{0,4},{1,5},{2,6},{3,7},{8,12},{9,13},{10,14},{11,15},{16,20},{17,... | collective-permute-start | bytes 198152 | tf_op jit(solution)/shard_map/ppermute | solution.py:15
  131.7 23.0 %collective-permute-start.10 = (bf16[1,18,16512]{2,1,0:T(8,128)(2,1)}, bf16[1,18,16512]{2,1,0:T(8,128)(2,1)}, u32[]{:S(2)}, u32[]{:S(2)}) collective-permute-start(bf16[1,18,16512]{2,1,0:T(8,128)(2,1)} %get-tuple-element.5), channel_id=1, source_target_pairs={{1,0},{2,1},{3,2},{5,4},{6,5},{7,6},{9,8},{10,9},{11,10},{13,12},{... | collective-permute-start | bytes 1783304 | tf_op jit(solution)/shard_map/ppermute | solution.py:16
  133.0 22.9 %collective-permute-start.11 = (bf16[1,18,16512]{2,1,0:T(8,128)(2,1)}, bf16[1,18,16512]{2,1,0:T(8,128)(2,1)}, u32[]{:S(2)}, u32[]{:S(2)}) collective-permute-start(bf16[1,18,16512]{2,1,0:T(8,128)(2,1)} %get-tuple-element.6), channel_id=1, source_target_pairs={{0,1},{1,2},{2,3},{4,5},{5,6},{6,7},{8,9},{9,10},{10,11},{12,13},{... | collective-permute-start | bytes 1783304 | tf_op jit(solution)/shard_map/ppermute | solution.py:15
  141.5 93.2 %all-reduce.2.cloned.1.call-start = ((), (), s32[]{:S(2)}) async-start(), calls=%async_computation.4 | async-start | bytes 524288 | tf_op jit(solution)/shard_map/psum | solution.py:100
  191.0 45.5 %copy-start.1 = (bf16[64,256]{1,0:T(8,128)(2,1)S(1)}, bf16[64,256]{1,0:T(8,128)(2,1)}, u32[]{:S(2)}) copy-start(bf16[64,256]{1,0:T(8,128)(2,1)} %param.9) | copy-start | bytes 98308
  (13 other events, 34.5 us)
Sparse Core Ops, SparseCore 0:
  24.6 27.1 reduce-scatter.2
  141.6 23.6 reduce-scatter.4
  179.7 54.9 all-reduce.1
where the time goes:
time: 244 us; the launch traced here: 243 us
  local copies, waits for them, and re-layouts  62.6 us (26%)
  other arithmetic  51.6 us (21%)
  waiting for transfers between devices  43.3 us (18%)
  starting transfers between devices  26.4 us (11%)
  matrix products  25.6 us (10%)
  blocking collectives  18.8 us (8%)
  between operations  14.7 us (6%)
    psum x1, waiting for transfers between devices, sum_gradients(): lax.psum(local_grads.astype(jnp.bfloat16), ('gy', 'gz')).astype(jnp.float32)  22.1 us
    convert_element_type x1, other arithmetic, per_device(): (grad_local + spectral_grad.reshape(planes, y_cells, merged)).astype(jnp....  21.6 us
    all_gather x2, blocking collectives, share_inverse(): segment = lax.all_gather(modes_share, 'gx', axis=0, tiled=True)  18.8 us
    mul x27, local copies, waits for them, and re-layouts, depthwise(): running = running + cut.astype(jnp.float32) * jnp.tile(tap_gain, x_cells)  18.6 us
    ppermute x6, starting transfers between devices, padded_2(): before = lax.ppermute(last, axis, up)  15.6 us
    convert_element_type x1, other arithmetic, per_device(): depthwise(padded, depth_weight, False, x_cells, channels)  14.8 us
    ppermute x6, waiting for transfers between devices, padded_2(): after = lax.ppermute(leading, axis, down)  11.2 us
    ppermute x6, starting transfers between devices, padded_2(): after = lax.ppermute(leading, axis, down)  10.7 us
  transfers between devices with their start and end apart: 15, of which 8 were waited for; matrix products, arithmetic and copies ran while one was open for 43% of the time, Pallas kernels for 0%

commit v1 on v0

--- a/solution.py
+++ b/solution.py
@@ -81,7 +81,36 @@
 
 
 def share_inverse(modes_share, cos_table, sin_table, channels):
-    segment = lax.all_gather(modes_share, "gx", axis=0, tiled=True)
+    a_now = lax.axis_size("gx")
+    arrivals = []
+    w1, e_next, everything = (a_now, lax.axis_index("gx"), modes_share.shape[0])
+    for at, t in enumerate(modes_share.shape):
+        arrivals.append(t * w1 if at == 0 else t)
+    out_arr = jnp.zeros(arrivals, modes_share.dtype)
+    v_next = parts_out = modes_share
+    it = 1
+    segment = lax.dynamic_update_slice_in_dim(out_arr, modes_share, e_next * everything, axis=0)
+    while it < w1 // 2 + 1:
+        fields = []
+        at = 0
+        while at < w1:
+            fields.append((at, (at + 1) % w1))
+            at += 1
+        v_next = lax.ppermute(v_next, axis_name="gx", perm=fields)
+        segment = lax.dynamic_update_slice_in_dim(
+            segment, v_next, (e_next - it) % w1 * everything, axis=0
+        )
+        if 2 * it < w1:
+            all_blocks = []
+            at = 0
+            while at < w1:
+                all_blocks.append((at, (at - 1) % w1))
+                at += 1
+            parts_out = lax.ppermute(parts_out, "gx", all_blocks)
+            segment = lax.dynamic_update_slice_in_dim(
+                segment, parts_out, (e_next + it) % w1 * everything, axis=0
+            )
+        it += 1
     running = jnp.einsum(
         "krc,xk->rxc", segment[:, :, :channels], cos_table, preferred_element_type=jnp.float32
     )

time: 244 us -> 267 us (1.094)
  waiting for transfers between devices: 43.3 us -> 77.2 us
  blocking collectives: 18.8 us -> 0 us
  starting transfers between devices: 26.4 us -> 33.4 us
    psum x1, waiting for transfers between devices: 22.1 us -> 48.3 us  [sum_gradients(): lax.psum(local_grads.astype(jnp.bfloat16), ('gy', 'gz')).astype(jnp.float32)]
    all_gather x2 -> x0, blocking collectives: 18.8 us -> none  [share_inverse(): segment = lax.all_gather(modes_share, 'gx', axis=0, tiled=True)]
    reduce_scatter x2, waiting for transfers between devices: 5.44 us -> 14.8 us  [share_terms(): lax.psum_scatter(jnp.concatenate([real_part, imag_part], axis=2), 'gx', s...]
    ppermute x0 -> x6, waiting for transfers between devices: none -> 7.23 us  [the longest x4 6.37 us: share_inverse(): v_next = lax.ppermute(v_next, axis_name='gx', perm=fields)]
    mul x27, local copies, waits for them, and re-layouts: 18.6 us -> 11.5 us  [depthwise(): running = running + cut.astype(jnp.float32) * jnp.tile(tap_gain, x_cells)]
    ppermute x0 -> x6, starting transfers between devices: none -> 6.43 us  [the longest x2 3.82 us: share_inverse(): parts_out = lax.ppermute(parts_out, 'gx', all_blocks)]
    ppermute x6, waiting for transfers between devices: 11.2 us -> 5.88 us  [padded_2(): after = lax.ppermute(leading, axis, down)]
    dynamic_update_slice x0 -> x8, local copies, waits for them, and re-layouts: none -> 5.28 us  [the longest x4 3.03 us: share_inverse(): lax.dynamic_update_slice_in_dim(segment, v_next, (e_next - it) % w1 * eve...]
  transfers between devices with their start and end apart: 15 -> 21, of which waited for: 8 -> 8; matrix products, arithmetic and copies ran while one was open for 43% -> 28% of each run, Pallas kernels for 0% -> 0%
where the time goes in v1:
time: 267 us; the launch traced here: 266 us
  waiting for transfers between devices  77.2 us (29%)
  local copies, waits for them, and re-layouts  61.6 us (23%)
  other arithmetic  51.9 us (19%)
  starting transfers between devices  33.4 us (13%)
  matrix products  27.2 us (10%)
  between operations  14.9 us (6%)
    psum x1, waiting for transfers between devices, sum_gradients(): lax.psum(local_grads.astype(jnp.bfloat16), ('gy', 'gz')).astype(jnp.float32)  48.3 us
    convert_element_type x1, other arithmetic, per_device(): (grad_local + spectral_grad.reshape(planes, y_cells, merged)).astype(jnp....  21.2 us
    ppermute x6, starting transfers between devices, padded_2(): before = lax.ppermute(last, axis, up)  17.6 us
    reduce_scatter x2, waiting for transfers between devices, share_terms(): lax.psum_scatter(jnp.concatenate([real_part, imag_part], axis=2), 'gx', s...  14.8 us
    convert_element_type x1, other arithmetic, per_device(): depthwise(padded, depth_weight, False, x_cells, channels)  14.7 us
    mul x27, local copies, waits for them, and re-layouts, depthwise(): running = running + cut.astype(jnp.float32) * jnp.tile(tap_gain, x_cells)  11.5 us
    ppermute x6, starting transfers between devices, padded_2(): after = lax.ppermute(leading, axis, down)  9.24 us
    concatenate x4, other arithmetic, padded_2(): value = jnp.concatenate([before, value, after], axis=dim)  7.92 us
  transfers between devices with their start and end apart: 21, of which 8 were waited for; matrix products, arithmetic and copies ran while one was open for 28% of the time, Pallas kernels for 0%

profile of v1, /device:TPU:0, one launch (start us, length us, event | category | flops | bytes accessed | tf_op | source)
XLA Modules:
  0.0 266.3 jit_solution(9782478810152942613)
XLA Ops:
  8.0 2.9 %collective-permute-start = (bf16[2,16,64]{2,1,0:T(8,128)(2,1)S(1)}, bf16[2,16,64]{2,1,0:T(8,128)(2,1)S(1)}, u32[]{:S(2)}, u32[]{:S(2)}) collective-permute-start(bf16[2,16,64]{2,1,0:T(8,128)(2,1)S(1)} %get-tuple-element.22), channel_id=1, source_target_pairs={{0,8},{8,16},{16,24},{24,0},{1,9},{9,17},{17,25},{25,1},{2,10},{10... | collective-permute-start | bytes 12296 | tf_op jit(solution)/shard_map/ppermute | solution.py:15
  12.0 3.0 %reshape.69 = bf16[32,256,64]{2,1,0:T(8,128)(2,1)S(1)} reshape(bf16[2,16,16384]{2,1,0:T(8,128)(2,1)} %param.7) | data formatting | bytes 2097152 | tf_op jit(solution)/shard_map/reshape | solution.py:156
  15.0 1.4 fusion.48
  16.4 1.3 fusion.51
  17.7 2.9 %concatenate.105 = bf16[2,16,16512]{2,1,0:T(8,128)(2,1)S(1)} concatenate(bf16[2,16,64]{2,1,0:T(8,128)(2,1)S(1)} %collective-permute-done, bf16[2,16,16384]{2,1,0:T(8,128)(2,1)} %param.7, bf16[2,16,64]{2,1,0:T(8,128)(2,1)S(1)} %collective-permute-done.1), dimensions={2} | concatenate | bytes 2113536 | tf_op jit(solution)/shard_map/concatenate | solution.py:17
  21.5 1.3 collective-permute-start.3
  22.8 3.0 %collective-permute-start.2 = (bf16[2,1,16512]{2,1,0:T(2,128)(2,1)}, bf16[2,1,16512]{2,1,0:T(2,128)(2,1)S(1)}, u32[]{:S(2)}, u32[]{:S(2)}) collective-permute-start(bf16[2,1,16512]{2,1,0:T(2,128)(2,1)} %get-tuple-element.17), channel_id=1, source_target_pairs={{0,4},{1,5},{2,6},{3,7},{8,12},{9,13},{10,14},{11,15},{16,20},{17,... | collective-permute-start | bytes 198152 | tf_op jit(solution)/shard_map/ppermute | solution.py:15
  27.0 3.3 %reshape.101 = f32[32,256,64]{2,1,0:T(8,128)} reshape(bf16[2,16,16384]{2,1,0:T(8,128)(2,1)S(1)} %copy-done.16) | data formatting | bytes 3145728 | tf_op jit(solution)/shard_map/convert_element_type | solution.py:169
  30.3 3.8 %copy.31 = f32[32,256,64]{1,2,0:T(8,128)} copy(f32[32,256,64]{2,1,0:T(8,128)} %reshape.101) | data formatting | bytes 4194304 | tf_op jit(solution)/shard_map/convert_element_type | solution.py:169
  34.9 1.2 fusion.95
  36.2 4.8 %collective-permute-start.4 = (bf16[1,18,16512]{2,1,0:T(8,128)(2,1)}, bf16[1,18,16512]{2,1,0:T(8,128)(2,1)}, u32[]{:S(2)}, u32[]{:S(2)}) collective-permute-start(bf16[1,18,16512]{2,1,0:T(8,128)(2,1)} %get-tuple-element.9), channel_id=1, source_target_pairs={{0,1},{1,2},{2,3},{4,5},{5,6},{6,7},{8,9},{9,10},{10,11},{12,13},{... | collective-permute-start | bytes 1783304 | tf_op jit(solution)/shard_map/ppermute | solution.py:15
  41.0 1.5 collective-permute-start.5
  56.9 5.0 %collective-permute-done.5 = bf16[1,18,16512]{2,1,0:T(8,128)(2,1)} collective-permute-done((bf16[1,18,16512]{2,1,0:T(8,128)(2,1)}, bf16[1,18,16512]{2,1,0:T(8,128)(2,1)}, u32[]{:S(2)}, u32[]{:S(2)}) %collective-permute-start.5) | collective-permute-done | bytes 594464 | tf_op jit(solution)/shard_map/ppermute | solution.py:16
  61.9 2.8 %maximum_maximum_fusion = (bf16[3,18,16512]{2,1,0:T(8,128)(2,1)S(1)}, bf16[3,18,16512]{2,1,0:T(8,128)(2,1)S(1)}) fusion(bf16[2,1,16512]{2,1,0:T(2,128)(2,1)S(1)} %collective-permute-done.3, bf16[2,16,16512]{2,1,0:T(8,128)(2,1)S(1)} %concatenate.105, bf16[2,1,16512]{2,1,0:T(2,128)(2,1)S(1)} %collective-permute-done.2, ...), kind=kLoop, calls=%fused_computation.12 | loop fusion | flops 14266368 | bytes 5944320 | tf_op jit(solution)/shard_map/concatenate | solution.py:17
  65.0 14.7 %add_convert_fusion.1 = bf16[2,16,16384]{2,1,0:T(8,128)(2,1)} fusion(bf16[2,16,16384]{2,1,0:T(8,128)(2,1)S(1)} %copy-done.3, bf16[2,16,16512]{2,1,0:T(8,128)(2,1)S(1)} %concatenate.105, bf16[2,1,16512]{2,1,0:T(2,128)(2,1)S(1)} %collective-permute-done.3, bf16[2,1,16512]{2,1,0:T(2,128)(2,1)S(1)} %collective-permute-done.2, ...), kind=kLoop, calls=%fused_computation.35 | loop fusion | flops 55050240 | bytes 23938048 | tf_op jit(solution)/shard_map/convert_element_type | solution.py:148
  79.7 3.0 %reshape.67 = bf16[8192,64]{1,0:T(8,128)(2,1)S(1)} reshape(bf16[2,16,16384]{2,1,0:T(8,128)(2,1)} %add_convert_fusion.1) | data formatting | bytes 2097152 | tf_op jit(solution)/shard_map/reshape | solution.py:149
  84.0 3.3 %copy-done.2 = f32[8192,256]{1,0:T(8,128)} copy-done((f32[8192,256]{1,0:T(8,128)}, f32[8192,256]{1,0:T(8,128)S(1)}, u32[]{:S(2)}) %copy-start.2) | copy-done | bytes 8388632
  87.3 3.3 %fusion.5 = f32[8192,64]{0,1:T(8,128)} fusion(bf16[256,64]{0,1:T(8,128)(2,1)S(1)} %copy-done.47, f32[8192,256]{1,0:T(8,128)S(1)} %fusion.100), kind=kOutput, calls=%fused_computation.10 | convolution fusion | flops 278921216 | bytes 10518528 | tf_op jit(solution)/shard_map/dot_general | solution.py:152
  92.5 2.3 collective-permute-start.7
  95.0 2.1 collective-permute-done.6
  98.1 4.2 %collective-permute-done.8 = bf16[8,32,128]{2,1,0:T(8,128)(2,1)S(1)} collective-permute-done((bf16[8,32,128]{2,1,0:T(8,128)(2,1)S(1)}, bf16[8,32,128]{2,1,0:T(8,128)(2,1)S(1)}, u32[]{:S(2)}, u32[]{:S(2)}) %collective-permute-start.8) | collective-permute-done | bytes 65568 | tf_op jit(solution)/shard_map/ppermute | solution.py:99
  103.2 3.8 %fusion.11 = (bf16[32,256,64]{1,2,0:T(8,128)(2,1)S(1)}, bf16[32,256,64]{1,2,0:T(8,128)(2,1)}) fusion(f32[32,256,64]{1,2,0:T(8,128)S(1)} %copy-done.5, f32[256,32,64]{0,2,1:T(8,128)S(1)} %fusion.28, bf16[32,32,128]{2,0,1:T(8,128)(2,1)S(1)} %copy_dynamic-update-slice_fusion, f32[32]{0:T(128)S(1)} %fusion.67, s32[256]{0:T(256)S(1)} %iota_add_fusion, ...), kind=kOutput, calls=%fused_computation.29 | convolution fusion | flops 41041920 | bytes 8651904 | tf_op jit(solution)/shard_map/krc,xk->rxc/dot_general | solution.py:114
  107.0 1.4 fusion.53
  108.5 7.9 %convolution_convert_fusion = bf16[8192,64]{0,1:T(8,128)(2,1)S(1)} fusion(bf16[64,256]{1,0:T(8,128)(2,1)S(1)} %copy-done, bf16[8192,64]{0,1:T(8,128)(2,1)S(1)} %bitcast.128, bf16[256,64]{0,1:T(8,128)(2,1)} %param.10, f32[8192,256]{1,0:T(8,128)} %copy-done.2), kind=kOutput, calls=%fused_computation.3 | convolution fusion | flops 558366720 | bytes 10551296 | tf_op jit(solution)/shard_map/dot_general | solution.py:177
  116.4 1.8 copy.33
  118.1 2.9 %reshape.72 = bf16[2,16,16384]{2,1,0:T(8,128)(2,1)S(1)} reshape(bf16[8192,64]{1,0:T(8,128)(2,1)} %copy.33) | data formatting | bytes 2097152 | tf_op jit(solution)/shard_map/reshape | solution.py:180
  121.2 2.9 %collective-permute-start.10 = (bf16[2,16,64]{2,1,0:T(8,128)(2,1)S(1)}, bf16[2,16,64]{2,1,0:T(8,128)(2,1)S(1)}, u32[]{:S(2)}, u32[]{:S(2)}) collective-permute-start(bf16[2,16,64]{2,1,0:T(8,128)(2,1)S(1)} %get-tuple-element.19), channel_id=1, source_target_pairs={{8,0},{16,8},{24,16},{0,24},{9,1},{17,9},{25,17},{1,25},{10,2},{18... | collective-permute-start | bytes 12296 | tf_op jit(solution)/shard_map/ppermute | solution.py:16
  124.1 1.4 fusion.56
  125.6 1.8 copy.30
  127.3 3.7 %reshape.70 = bf16[2,16,16384]{2,1,0:T(8,128)(2,1)} reshape(bf16[32,256,64]{2,1,0:T(8,128)(2,1)} %copy.30) | data formatting | bytes 2097152 | tf_op jit(solution)/shard_map/reshape | solution.py:167
  132.4 1.3 collective-permute-start.11
  133.7 1.3 collective-permute-start.12
  138.5 1.3 collective-permute-start.13
  139.8 5.5 %collective-permute-start.14 = (bf16[1,18,16512]{2,1,0:T(8,128)(2,1)S(1)}, bf16[1,18,16512]{2,1,0:T(8,128)(2,1)}, u32[]{:S(2)}, u32[]{:S(2)}) collective-permute-start(bf16[1,18,16512]{2,1,0:T(8,128)(2,1)S(1)} %get-tuple-element.8), channel_id=1, source_target_pairs={{0,1},{1,2},{2,3},{4,5},{5,6},{6,7},{8,9},{9,10},{10,11},{12,13},{... | collective-permute-start | bytes 1783304 | tf_op jit(solution)/shard_map/ppermute | solution.py:15
  145.3 14.8 %reduce-scatter.5.cloned.1.call-done = f32[8,32,128]{2,0,1:T(8,128)} async-done(((f32[32,32,128]{2,0,1:T(8,128)}), f32[8,32,128]{2,0,1:T(8,128)}) %reduce-scatter.5.cloned.1.call-update) | async-done | bytes 131088 | tf_op jit(solution)/shard_map/reduce_scatter | solution.py:78
  162.7 1.4 collective-permute-start.15
  166.3 3.9 %pad_maximum_fusion.1 = (bf16[3,18,16512]{2,1,0:T(8,128)(2,1)S(1)}, bf16[3,18,16512]{2,1,0:T(8,128)(2,1)}) fusion(bf16[1,18,16512]{2,1,0:T(8,128)(2,1)} %copy-done.17, bf16[2,1,16512]{2,1,0:T(2,128)(2,1)} %copy-done.15, bf16[2,16,16512]{2,1,0:T(8,128)(2,1)S(1)} %concatenate.117, bf16[2,1,16512]{2,1,0:T(2,128)(2,1)} %copy-done.14, ...), kind=kLoop, calls=%fused_computation.14 | loop fusion | flops 14266368 | bytes 5944320 | tf_op jit(solution)/shard_map/concatenate | solution.py:17
  170.2 1.5 collective-permute-start.16
  172.3 48.3 %all-reduce.2.cloned.1.call-done = bf16[2,8,64,64]{3,2,1,0:T(8,128)(2,1)} async-done(((bf16[2,8,64,64]{3,2,1,0:T(8,128)(2,1)}), bf16[2,8,64,64]{3,2,1,0:T(8,128)(2,1)}) %all-reduce.2.cloned.1.call-update) | async-done | bytes 131088 | tf_op jit(solution)/shard_map/psum | solution.py:129
  220.6 1.8 convert_element_type.381
  222.3 1.5 constant_dynamic-update-slice_fusion.2
  223.8 1.5 constant_dynamic-update-slice_fusion.1
  225.3 1.5 constant_dynamic-update-slice_fusion
  226.8 2.0 fusion.25
  228.8 2.0 add_bitcast_fusion
  230.8 3.8 %copy.36 = f32[32,256,64]{2,1,0:T(8,128)} copy(f32[32,256,64]{1,2,0:T(8,128)} %add_bitcast_fusion) | data formatting | bytes 4194304 | tf_op jit(solution)/shard_map/add | solution.py:117
  234.6 3.9 %reshape.73 = f32[2,16,16384]{2,1,0:T(8,128)} reshape(f32[32,256,64]{2,1,0:T(8,128)} %copy.36) | data formatting | bytes 4194304 | tf_op jit(solution)/shard_map/reshape | solution.py:190
  238.5 21.2 %add_convert_fusion = bf16[2,16,16384]{2,1,0:T(8,128)(2,1)} fusion(f32[2,16,16384]{2,1,0:T(8,128)} %reshape.73, bf16[2,16,16384]{2,1,0:T(8,128)(2,1)} %copy-done.4, bf16[2,16,16512]{2,1,0:T(8,128)(2,1)S(1)} %concatenate.117, bf16[2,1,16512]{2,1,0:T(2,128)(2,1)} %copy-done.14, bf16[2,1,16512]{2,1,0:T(2,128)(2,1)} %copy-done.15, ...), kind=kLoop, calls=%fused_computation.31 | loop fusion | flops 55574528 | bytes 26035200 | tf_op jit(solution)/shard_map/convert_element_type | solution.py:190
  (209 shorter events, 33.9 us)
Async XLA Ops:
  7.2 75.6 %copy-start = (bf16[64,256]{1,0:T(8,128)(2,1)S(1)}, bf16[64,256]{1,0:T(8,128)(2,1)}, u32[]{:S(2)}) copy-start(bf16[64,256]{1,0:T(8,128)(2,1)} %param.9) | copy-start | bytes 98308
  7.2 83.5 %reduce-scatter.3.cloned.1.call-start = ((), (), s32[]{:S(2)}) async-start(), calls=%async_computation.2 | async-start | bytes 655360 | tf_op jit(solution)/shard_map/reduce_scatter | solution.py:78
  8.0 9.7 %collective-permute-start = (bf16[2,16,64]{2,1,0:T(8,128)(2,1)S(1)}, bf16[2,16,64]{2,1,0:T(8,128)(2,1)S(1)}, u32[]{:S(2)}, u32[]{:S(2)}) collective-permute-start(bf16[2,16,64]{2,1,0:T(8,128)(2,1)S(1)} %get-tuple-element.22), channel_id=1, source_target_pairs={{0,8},{8,16},{16,24},{24,0},{1,9},{9,17},{17,25},{25,1},{2,10},{10... | collective-permute-start | bytes 12296 | tf_op jit(solution)/shard_map/ppermute | solution.py:15
  11.0 6.8 %collective-permute-start.1 = (bf16[2,16,64]{2,1,0:T(8,128)(2,1)S(1)}, bf16[2,16,64]{2,1,0:T(8,128)(2,1)S(1)}, u32[]{:S(2)}, u32[]{:S(2)}) collective-permute-start(bf16[2,16,64]{2,1,0:T(8,128)(2,1)S(1)} %get-tuple-element.21), channel_id=1, source_target_pairs={{8,0},{16,8},{24,16},{0,24},{9,1},{17,9},{25,17},{1,25},{10,2},{18... | collective-permute-start | bytes 12296 | tf_op jit(solution)/shard_map/ppermute | solution.py:16
  17.7 9.3 %copy-start.16 = (bf16[2,16,16384]{2,1,0:T(8,128)(2,1)S(1)}, bf16[2,16,16384]{2,1,0:T(8,128)(2,1)}, u32[]{:S(2)}) copy-start(bf16[2,16,16384]{2,1,0:T(8,128)(2,1)} %param.13) | copy-start | bytes 3145732
  21.5 12.8 %collective-permute-start.3 = (bf16[2,1,16512]{2,1,0:T(2,128)(2,1)}, bf16[2,1,16512]{2,1,0:T(2,128)(2,1)S(1)}, u32[]{:S(2)}, u32[]{:S(2)}) collective-permute-start(bf16[2,1,16512]{2,1,0:T(2,128)(2,1)} %get-tuple-element.18), channel_id=1, source_target_pairs={{4,0},{5,1},{6,2},{7,3},{12,8},{13,9},{14,10},{15,11},{20,16},{21,... | collective-permute-start | bytes 198152 | tf_op jit(solution)/shard_map/ppermute | solution.py:16
  22.8 11.5 %collective-permute-start.2 = (bf16[2,1,16512]{2,1,0:T(2,128)(2,1)}, bf16[2,1,16512]{2,1,0:T(2,128)(2,1)S(1)}, u32[]{:S(2)}, u32[]{:S(2)}) collective-permute-start(bf16[2,1,16512]{2,1,0:T(2,128)(2,1)} %get-tuple-element.17), channel_id=1, source_target_pairs={{0,4},{1,5},{2,6},{3,7},{8,12},{9,13},{10,14},{11,15},{16,20},{17,... | collective-permute-start | bytes 198152 | tf_op jit(solution)/shard_map/ppermute | solution.py:15
  26.9 133.2 %reduce-scatter.5.cloned.1.call-start = ((), (), s32[]{:S(2)}) async-start(), calls=%async_computation.3 | async-start | bytes 655360 | tf_op jit(solution)/shard_map/reduce_scatter | solution.py:78
  36.2 20.7 %collective-permute-start.4 = (bf16[1,18,16512]{2,1,0:T(8,128)(2,1)}, bf16[1,18,16512]{2,1,0:T(8,128)(2,1)}, u32[]{:S(2)}, u32[]{:S(2)}) collective-permute-start(bf16[1,18,16512]{2,1,0:T(8,128)(2,1)} %get-tuple-element.9), channel_id=1, source_target_pairs={{0,1},{1,2},{2,3},{4,5},{5,6},{6,7},{8,9},{9,10},{10,11},{12,13},{... | collective-permute-start | bytes 1783304 | tf_op jit(solution)/shard_map/ppermute | solution.py:15
  41.0 20.9 %collective-permute-start.5 = (bf16[1,18,16512]{2,1,0:T(8,128)(2,1)}, bf16[1,18,16512]{2,1,0:T(8,128)(2,1)}, u32[]{:S(2)}, u32[]{:S(2)}) collective-permute-start(bf16[1,18,16512]{2,1,0:T(8,128)(2,1)} %get-tuple-element.10), channel_id=1, source_target_pairs={{1,0},{2,1},{3,2},{5,4},{6,5},{7,6},{9,8},{10,9},{11,10},{13,12},{... | collective-permute-start | bytes 1783304 | tf_op jit(solution)/shard_map/ppermute | solution.py:16
  42.7 22.0 %copy-start.18 = (f32[16384]{0:T(1024)}, f32[16384]{0:T(1024)S(1)}, u32[]{:S(2)}) copy-start(f32[16384]{0:T(1024)S(1)} %mul.634) | copy-start | bytes 196612
  42.9 21.8 %copy-start.19 = (f32[16384]{0:T(1024)}, f32[16384]{0:T(1024)S(1)}, u32[]{:S(2)}) copy-start(f32[16384]{0:T(1024)S(1)} %mul.631) | copy-start | bytes 196612
  43.0 21.7 %copy-start.20 = (f32[16384]{0:T(1024)}, f32[16384]{0:T(1024)S(1)}, u32[]{:S(2)}) copy-start(f32[16384]{0:T(1024)S(1)} %mul.628) | copy-start | bytes 196612
  43.1 21.6 %copy-start.21 = (f32[16384]{0:T(1024)}, f32[16384]{0:T(1024)S(1)}, u32[]{:S(2)}) copy-start(f32[16384]{0:T(1024)S(1)} %mul.625) | copy-start | bytes 196612
  43.2 21.5 %copy-start.22 = (f32[16384]{0:T(1024)}, f32[16384]{0:T(1024)S(1)}, u32[]{:S(2)}) copy-start(f32[16384]{0:T(1024)S(1)} %mul.622) | copy-start | bytes 196612
  43.3 21.4 %copy-start.23 = (f32[16384]{0:T(1024)}, f32[16384]{0:T(1024)S(1)}, u32[]{:S(2)}) copy-start(f32[16384]{0:T(1024)S(1)} %mul.619) | copy-start | bytes 196612
  43.4 21.3 %copy-start.24 = (f32[16384]{0:T(1024)}, f32[16384]{0:T(1024)S(1)}, u32[]{:S(2)}) copy-start(f32[16384]{0:T(1024)S(1)} %mul.616) | copy-start | bytes 196612
  43.5 21.2 %copy-start.25 = (f32[16384]{0:T(1024)}, f32[16384]{0:T(1024)S(1)}, u32[]{:S(2)}) copy-start(f32[16384]{0:T(1024)S(1)} %mul.613) | copy-start | bytes 196612
  43.7 21.1 %copy-start.26 = (f32[16384]{0:T(1024)}, f32[16384]{0:T(1024)S(1)}, u32[]{:S(2)}) copy-start(f32[16384]{0:T(1024)S(1)} %mul.610) | copy-start | bytes 196612
  43.8 21.0 %copy-start.27 = (f32[16384]{0:T(1024)}, f32[16384]{0:T(1024)S(1)}, u32[]{:S(2)}) copy-start(f32[16384]{0:T(1024)S(1)} %mul.607) | copy-start | bytes 196612
  43.9 20.9 %copy-start.28 = (f32[16384]{0:T(1024)}, f32[16384]{0:T(1024)S(1)}, u32[]{:S(2)}) copy-start(f32[16384]{0:T(1024)S(1)} %mul.604) | copy-start | bytes 196612
  55.8 9.0 %copy-start.3 = (bf16[2,16,16384]{2,1,0:T(8,128)(2,1)S(1)}, bf16[2,16,16384]{2,1,0:T(8,128)(2,1)}, u32[]{:S(2)}) copy-start(bf16[2,16,16384]{2,1,0:T(8,128)(2,1)} %param.7) | copy-start | bytes 3145732
  55.8 9.0 %copy-start.29 = (f32[16384]{0:T(1024)S(1)}, f32[16384]{0:T(1024)}, u32[]{:S(2)}) copy-start(f32[16384]{0:T(1024)} %mul.601) | copy-start | bytes 196612
  55.8 9.0 %copy-start.30 = (f32[16384]{0:T(1024)S(1)}, f32[16384]{0:T(1024)}, u32[]{:S(2)}) copy-start(f32[16384]{0:T(1024)} %mul.598) | copy-start | bytes 196612
  55.8 9.0 %copy-start.31 = (f32[16384]{0:T(1024)S(1)}, f32[16384]{0:T(1024)}, u32[]{:S(2)}) copy-start(f32[16384]{0:T(1024)} %mul.595) | copy-start | bytes 196612
  55.8 9.0 %copy-start.32 = (f32[16384]{0:T(1024)S(1)}, f32[16384]{0:T(1024)}, u32[]{:S(2)}) copy-start(f32[16384]{0:T(1024)} %mul.592) | copy-start | bytes 196612
  55.8 9.0 %copy-start.33 = (f32[16384]{0:T(1024)S(1)}, f32[16384]{0:T(1024)}, u32[]{:S(2)}) copy-start(f32[16384]{0:T(1024)} %mul.589) | copy-start | bytes 196612
  55.8 9.0 %copy-start.34 = (f32[16384]{0:T(1024)S(1)}, f32[16384]{0:T(1024)}, u32[]{:S(2)}) copy-start(f32[16384]{0:T(1024)} %mul.586) | copy-start | bytes 196612
  55.8 9.0 %copy-start.35 = (f32[16384]{0:T(1024)S(1)}, f32[16384]{0:T(1024)}, u32[]{:S(2)}) copy-start(f32[16384]{0:T(1024)} %mul.583) | copy-start | bytes 196612
  55.8 9.0 %copy-start.36 = (f32[16384]{0:T(1024)S(1)}, f32[16384]{0:T(1024)}, u32[]{:S(2)}) copy-start(f32[16384]{0:T(1024)} %mul.580) | copy-start | bytes 196612
  90.7 12.6 %copy-start.5 = (f32[32,256,64]{1,2,0:T(8,128)S(1)}, f32[32,256,64]{1,2,0:T(8,128)}, u32[]{:S(2)}) copy-start(f32[32,256,64]{1,2,0:T(8,128)} %copy.31) | copy-start | bytes 6291460
  91.7 11.5 %copy-start.44 = (bf16[8,32,128]{2,0,1:T(8,128)(2,1)}, bf16[8,32,128]{2,0,1:T(8,128)(2,1)S(1)}, u32[]{:S(2)}) copy-start(bf16[8,32,128]{2,0,1:T(8,128)(2,1)S(1)} %convert_element_type.341) | copy-start | bytes 196612
  91.9 5.2 %collective-permute-start.6 = (bf16[8,32,128]{2,1,0:T(8,128)(2,1)S(1)}, bf16[8,32,128]{2,1,0:T(8,128)(2,1)S(1)}, u32[]{:S(2)}, u32[]{:S(2)}) collective-permute-start(bf16[8,32,128]{2,1,0:T(8,128)(2,1)S(1)} %convolution_convert_fusion.1), channel_id=1, source_target_pairs={{0,8},{8,16},{16,24},{24,0},{1,9},{9,17},{17,25},{25,1},{2,10},{10... | collective-permute-start | bytes 196616 | tf_op jit(solution)/shard_map/ppermute | solution.py:99
  92.5 5.5 %collective-permute-start.7 = (bf16[8,32,128]{2,1,0:T(8,128)(2,1)S(1)}, bf16[8,32,128]{2,1,0:T(8,128)(2,1)S(1)}, u32[]{:S(2)}, u32[]{:S(2)}) collective-permute-start(bf16[8,32,128]{2,1,0:T(8,128)(2,1)S(1)} %convolution_convert_fusion.1), channel_id=1, source_target_pairs={{0,24},{8,0},{16,8},{24,16},{1,25},{9,1},{17,9},{25,17},{2,26},{10... | collective-permute-start | bytes 196616 | tf_op jit(solution)/shard_map/ppermute | solution.py:109
  97.1 5.2 %collective-permute-start.8 = (bf16[8,32,128]{2,1,0:T(8,128)(2,1)S(1)}, bf16[8,32,128]{2,1,0:T(8,128)(2,1)S(1)}, u32[]{:S(2)}, u32[]{:S(2)}) collective-permute-start(bf16[8,32,128]{2,1,0:T(8,128)(2,1)S(1)} %collective-permute-done.6), channel_id=1, source_target_pairs={{0,8},{8,16},{16,24},{24,0},{1,9},{9,17},{17,25},{25,1},{2,10},{10... | collective-permute-start | bytes 196616 | tf_op jit(solution)/shard_map/ppermute | solution.py:99
  121.1 9.9 %copy-start.4 = (bf16[2,16,16384]{2,1,0:T(8,128)(2,1)}, bf16[2,16,16384]{2,1,0:T(8,128)(2,1)S(1)}, u32[]{:S(2)}) copy-start(bf16[2,16,16384]{2,1,0:T(8,128)(2,1)S(1)} %reshape.72) | copy-start | bytes 3145732
  121.2 9.8 %collective-permute-start.9 = (bf16[2,16,64]{2,1,0:T(8,128)(2,1)S(1)}, bf16[2,16,64]{2,1,0:T(8,128)(2,1)S(1)}, u32[]{:S(2)}, u32[]{:S(2)}) collective-permute-start(bf16[2,16,64]{2,1,0:T(8,128)(2,1)S(1)} %get-tuple-element.20), channel_id=1, source_target_pairs={{0,8},{8,16},{16,24},{24,0},{1,9},{9,17},{17,25},{25,1},{2,10},{10... | collective-permute-start | bytes 12296 | tf_op jit(solution)/shard_map/ppermute | solution.py:15
  121.2 9.8 %collective-permute-start.10 = (bf16[2,16,64]{2,1,0:T(8,128)(2,1)S(1)}, bf16[2,16,64]{2,1,0:T(8,128)(2,1)S(1)}, u32[]{:S(2)}, u32[]{:S(2)}) collective-permute-start(bf16[2,16,64]{2,1,0:T(8,128)(2,1)S(1)} %get-tuple-element.19), channel_id=1, source_target_pairs={{8,0},{16,8},{24,16},{0,24},{9,1},{17,9},{25,17},{1,25},{10,2},{18... | collective-permute-start | bytes 12296 | tf_op jit(solution)/shard_map/ppermute | solution.py:16
  132.4 3.7 %collective-permute-start.11 = (bf16[2,1,16512]{2,1,0:T(2,128)(2,1)S(1)}, bf16[2,1,16512]{2,1,0:T(2,128)(2,1)S(1)}, u32[]{:S(2)}, u32[]{:S(2)}) collective-permute-start(bf16[2,1,16512]{2,1,0:T(2,128)(2,1)S(1)} %get-tuple-element.16), channel_id=1, source_target_pairs={{0,4},{1,5},{2,6},{3,7},{8,12},{9,13},{10,14},{11,15},{16,20},{17,... | collective-permute-start | bytes 198152 | tf_op jit(solution)/shard_map/ppermute | solution.py:15
  133.7 3.2 %collective-permute-start.12 = (bf16[2,1,16512]{2,1,0:T(2,128)(2,1)S(1)}, bf16[2,1,16512]{2,1,0:T(2,128)(2,1)S(1)}, u32[]{:S(2)}, u32[]{:S(2)}) collective-permute-start(bf16[2,1,16512]{2,1,0:T(2,128)(2,1)S(1)} %get-tuple-element.15), channel_id=1, source_target_pairs={{4,0},{5,1},{6,2},{7,3},{12,8},{13,9},{14,10},{15,11},{20,16},{21,... | collective-permute-start | bytes 198152 | tf_op jit(solution)/shard_map/ppermute | solution.py:16
  136.0 84.5 %all-reduce.2.cloned.1.call-start = ((), (), s32[]{:S(2)}) async-start(), calls=%async_computation.4 | async-start | bytes 524288 | tf_op jit(solution)/shard_map/psum | solution.py:129
  137.5 26.6 %copy-start.45 = (bf16[8,32,128]{2,0,1:T(8,128)(2,1)S(1)}, bf16[8,32,128]{2,0,1:T(8,128)(2,1)}, u32[]{:S(2)}) copy-start(bf16[8,32,128]{2,0,1:T(8,128)(2,1)} %copy-done.44) | copy-start | bytes 196612
  138.5 26.9 %collective-permute-start.13 = (bf16[1,18,16512]{2,1,0:T(8,128)(2,1)}, bf16[1,18,16512]{2,1,0:T(8,128)(2,1)S(1)}, u32[]{:S(2)}, u32[]{:S(2)}) collective-permute-start(bf16[1,18,16512]{2,1,0:T(8,128)(2,1)} %get-tuple-element.7), channel_id=1, source_target_pairs={{1,0},{2,1},{3,2},{5,4},{6,5},{7,6},{9,8},{10,9},{11,10},{13,12},{... | collective-permute-start | bytes 1783304 | tf_op jit(solution)/shard_map/ppermute | solution.py:16
  139.8 26.5 %collective-permute-start.14 = (bf16[1,18,16512]{2,1,0:T(8,128)(2,1)S(1)}, bf16[1,18,16512]{2,1,0:T(8,128)(2,1)}, u32[]{:S(2)}, u32[]{:S(2)}) collective-permute-start(bf16[1,18,16512]{2,1,0:T(8,128)(2,1)S(1)} %get-tuple-element.8), channel_id=1, source_target_pairs={{0,1},{1,2},{2,3},{4,5},{5,6},{6,7},{8,9},{9,10},{10,11},{12,13},{... | collective-permute-start | bytes 1783304 | tf_op jit(solution)/shard_map/ppermute | solution.py:15
  162.7 9.0 %collective-permute-start.15 = (bf16[8,32,128]{2,0,1:T(8,128)(2,1)}, bf16[8,32,128]{2,0,1:T(8,128)(2,1)}, u32[]{:S(2)}, u32[]{:S(2)}) collective-permute-start(bf16[8,32,128]{2,0,1:T(8,128)(2,1)} %get-tuple-element.4), channel_id=1, source_target_pairs={{0,8},{8,16},{16,24},{24,0},{1,9},{9,17},{17,25},{25,1},{2,10},{10... | collective-permute-start | bytes 196616 | tf_op jit(solution)/shard_map/ppermute | solution.py:99
  170.2 53.6 %collective-permute-start.16 = (bf16[8,32,128]{2,0,1:T(8,128)(2,1)}, bf16[8,32,128]{2,0,1:T(8,128)(2,1)}, u32[]{:S(2)}, u32[]{:S(2)}) collective-permute-start(bf16[8,32,128]{2,0,1:T(8,128)(2,1)} %get-tuple-element.4), channel_id=1, source_target_pairs={{0,24},{8,0},{16,8},{24,16},{1,25},{9,1},{17,9},{25,17},{2,26},{10... | collective-permute-start | bytes 196616 | tf_op jit(solution)/shard_map/ppermute | solution.py:109
  171.7 53.6 %collective-permute-start.17 = (bf16[8,32,128]{2,0,1:T(8,128)(2,1)}, bf16[8,32,128]{2,0,1:T(8,128)(2,1)}, u32[]{:S(2)}, u32[]{:S(2)}) collective-permute-start(bf16[8,32,128]{2,0,1:T(8,128)(2,1)} %collective-permute-done.15), channel_id=1, source_target_pairs={{0,8},{8,16},{16,24},{24,0},{1,9},{9,17},{17,25},{25,1},{2,10},{10... | collective-permute-start | bytes 196616 | tf_op jit(solution)/shard_map/ppermute | solution.py:99
  238.5 21.2 %copy-start.1 = (bf16[64,256]{1,0:T(8,128)(2,1)S(1)}, bf16[64,256]{1,0:T(8,128)(2,1)}, u32[]{:S(2)}) copy-start(bf16[64,256]{1,0:T(8,128)(2,1)} %param.9) | copy-start | bytes 98308
  (21 other events, 122.0 us)
Sparse Core Ops, SparseCore 0:
  27.0 25.5 reduce-scatter.2
  136.1 23.9 reduce-scatter.4
  165.6 54.9 all-reduce.1
